TPU v7x, 512 devices: a whole 4x4x16 slice. The times are simulated.
512 devices in a mesh: sub: 128 (over y, z, core), case: 4 (over x).
Axes of the slice: x: 4, y: 4, z: 16, core: 2. Of those that a mesh axis runs over, the one named last changes fastest.
Arguments:
- load_interior: float32 [128, 128, 4096], P('sub', None, 'case'), may hold values from -6 to 6
- load_boundary: float32 [128, 128, 1024], P('sub', None, 'case'), may hold values from -6 to 6
- cond_blocks: float32 [128, 128, 4096], P('sub', 'case'), may hold values from -0.25 to 0.25
- block_rows: int32 [128, 128], P('sub', 'case'), may hold values from 0 to 15
- block_cols: int32 [128, 128], P('sub', 'case'), may hold values from 0 to 63, as said below
- interface_maps: int32 [128, 7, 2, 1024], P('sub'), may hold values from 0 to 1023, as said below
- merge_maps: float32 [128, 7, 1024, 512], P('sub', None, 'case'), as said below
Outputs:
- leaf_loads: float32 [128, 1024, 128], P('sub', 'case')
- node_loads: float32 [128, 1024, 128], P('sub', 'case')
Inputs may be any that keep to these rules, and one draw needn't show every extreme that they name: `block_cols`: entry k of a substructure's row lies in [(k // 32) * 16, (k // 32 + 1) * 16); blocks may repeat. `interface_maps`: each row of 1024 entries is a permutation; at level index l, slots that agree in all but their lowest l + 1 bits hold equal entries. `merge_maps`: at level index l, slots that agree in all but their lowest l + 1 bits hold equal entries.
All inputs are finite; a program needn't handle non-finite values.
Results may differ from a plain program's by a relative error of at most 0.0003.
Values sent between devices are 32-bit elements; how exact they have to be, the bound alone decides.
No kernel may reach another device: no remote copies, remote signals or barrier semaphores. Data moves between devices by JAX's collectives and lax.ppermute only.
A program may use at most 64 MiB of HBM per device.

v0:
```python
import jax
import jax.numpy as jnp
from jax import lax
from jax.sharding import PartitionSpec as P

BLK = 64


def from_partner(value, axis, distance):
    mask = 2**distance
    pairs = [(source, source ^ mask) for source in range(lax.axis_size(axis))]
    return lax.ppermute(value, axis, pairs)


def to_row_quarters(value):
    return lax.all_to_all(value, "case", split_axis=0, concat_axis=1, tiled=True)


def on_device(
    load_interior, load_boundary, cond_blocks, block_rows, block_cols, interface_maps, merge_maps
):
    groups = lax.axis_size("case")
    local_rows = load_interior.shape[2]
    quarter = load_boundary.shape[2]
    full_rows = quarter * groups
    interior_rows = local_rows * groups
    block_size = BLK
    blocks = lax.all_gather(cond_blocks[0], "case", axis=0, tiled=True)
    rows_of_blocks = lax.all_gather(block_rows[0], "case", axis=0, tiled=True)
    cols_of_blocks = lax.all_gather(block_cols[0], "case", axis=0, tiled=True)
    block_count = blocks.shape[0]
    blocks = blocks.reshape(block_count, block_size, block_size)
    joined = jnp.concatenate([load_interior, load_boundary], axis=2)
    joined = lax.all_to_all(joined, "sub", split_axis=1, concat_axis=0, tiled=True)[:, 0, :]
    joined = lax.all_to_all(joined, "case", split_axis=0, concat_axis=1, tiled=True)
    num_cases = joined.shape[0]
    parts = joined.reshape(num_cases, groups, local_rows + quarter)
    interior = jnp.transpose(parts[:, :, :local_rows].reshape(num_cases, interior_rows))
    boundary = jnp.transpose(parts[:, :, local_rows:].reshape(num_cases, full_rows))
    pieces = jnp.take(
        interior.reshape(interior_rows // block_size, block_size, num_cases), cols_of_blocks, axis=0
    )
    products = jnp.einsum("krc,kcn->krn", blocks, pieces, precision=lax.Precision.HIGH)
    row_blocks = full_rows // block_size
    onehot = (rows_of_blocks[None, :] == jnp.arange(row_blocks, dtype=jnp.int32)[:, None]).astype(
        jnp.float32
    )
    summed = jnp.dot(
        onehot, products.reshape(block_count, block_size * num_cases), precision=lax.Precision.HIGH
    )
    leaf = boundary - summed.reshape(full_rows, num_cases)
    leaf_share = to_row_quarters(leaf)
    slot = lax.axis_index("sub")
    levels = lax.axis_size("sub").bit_length() - 1
    current = leaf
    nodes = jnp.zeros_like(leaf)
    for level in range(1, levels + 1):
        half = 1 << level - 1
        maps = interface_maps[0, level - 1]
        matrix = lax.all_gather(merge_maps[0, level - 1], "case", axis=0, tiled=True)
        shared_rows = matrix.shape[1]
        upper = slot // half % 2 == 1
        other = from_partner(current, "sub", level - 1)
        stacked = jnp.concatenate([current, other], axis=0)

        def left_index(index):
            return jnp.where(upper, index + full_rows, index)

        def right_index(index):
            return jnp.where(upper, index, index + full_rows)

        shared = jnp.take(stacked, left_index(maps[0, :shared_rows]), axis=0) + jnp.take(
            stacked, right_index(maps[1, :shared_rows]), axis=0
        )
        kept_index = jnp.concatenate(
            [left_index(maps[0, shared_rows:]), right_index(maps[1, shared_rows:])]
        )
        parent = jnp.take(stacked, kept_index, axis=0) - jnp.dot(
            matrix, shared, precision=lax.Precision.HIGH
        )
        is_node = slot % (2 * half) == half
        if level == levels:
            is_node = jnp.logical_or(is_node, slot == 0)
        nodes = jnp.where(is_node, parent, nodes)
        current = parent
    return (leaf_share[None], to_row_quarters(nodes)[None])


def solution(mesh):
    placed = (
        P("sub", None, "case"),
        P("sub", None, "case"),
        P("sub", "case", None),
        P("sub", "case"),
        P("sub", "case"),
        P("sub", None, None, None),
        P("sub", None, "case", None),
    )
    return jax.shard_map(
        on_device,
        mesh=mesh,
        in_specs=placed,
        out_specs=(P("sub", "case", None), P("sub", "case", None)),
        check_vma=False,
    )
```

profile of v0, /device:TPU:8, one launch (start us, length us, event | category | flops | bytes accessed | tf_op | source)
XLA Modules:
  0.0 363.9 jit_solution(5309197116855584580)
XLA Ops:
  9.6 3.9 %fusion.110 = (f32[1,1,256,512]{3,2,1,0:T(8,128)}, f32[1,1,256,512]{3,2,1,0:T(8,128)}, f32[1,1,256,512]{3,2,1,0:T(8,128)}, f32[1,1,256,512]{3,2,1,0:T(8,128)}, f...) fusion(f32[1,7,256,512]{3,2,1,0:T(8,128)} %param.17), kind=kLoop, calls=%fused_computation.216 | loop fusion | bytes 7340032 | tf_op jit(solution)/shard_map/slice | solution.py:60
  18.4 19.6 %all-to-all-start = ((f32[1,128,1280]{2,0,1:T(1,128)}), f32[1,128,1280]{2,0,1:T(1,128)S(1)}, u32[]{:S(2)}, u32[]{:S(2)}) async-start(f32[1,128,1280]{2,0,1:T(1,128)} %copy.232), calls=%async_computation | async-start | bytes 1310720 | tf_op jit(solution)/shard_map/all_to_all | solution.py:34
  40.9 9.0 %all-reduce.2 = (s32[128]{0:T(128)S(1)}, s32[128]{0:T(128)S(1)}) all-reduce(s32[128]{0:T(128)S(1)} %bitcast_dynamic-update-slice_fusion, s32[128]{0:T(128)S(1)} %bitcast_dynamic-update-slice_fusion.1), channel_id=3, replica_groups=mesh['sub'=128,'case'=4] {'case'}, use_global_device_ids=true, to_apply=%add.1 | all-reduce | flops 256 | bytes 2048 | tf_op jit(solution)/shard_map/all_gather | solution.py:30
  50.8 26.4 %all-to-all-done = f32[1,128,1280]{2,0,1:T(1,128)S(1)} async-done(((f32[1,128,1280]{2,0,1:T(1,128)}), f32[1,128,1280]{2,0,1:T(1,128)S(1)}, u32[]{:S(2)}, u32[]{:S(2)}) %all-to-all-start) | async-done | bytes 655392 | tf_op jit(solution)/shard_map/all_to_all | solution.py:34
  78.2 4.3 %all-to-all-start.1 = ((f32[4,32,1280]{2,1,0:T(8,128)}), f32[4,32,1280]{2,1,0:T(8,128)S(1)}, u32[]{:S(2)}, u32[]{:S(2)}) async-start(f32[4,32,1280]{2,1,0:T(8,128)} %bitcast.67), calls=%async_computation.1 | async-start | bytes 1310720 | tf_op jit(solution)/shard_map/all_to_all | solution.py:35
  82.5 18.3 %all-to-all-done.1 = f32[4,32,1280]{2,1,0:T(8,128)S(1)} async-done(((f32[4,32,1280]{2,1,0:T(8,128)}), f32[4,32,1280]{2,1,0:T(8,128)S(1)}, u32[]{:S(2)}, u32[]{:S(2)}) %all-to-all-start.1) | async-done | bytes 655392 | tf_op jit(solution)/shard_map/all_to_all | solution.py:35
  103.9 5.6 %copy.237 = f32[1,128,4096]{1,2,0:T(8,128)} copy(f32[1,128,4096]{2,0,1:T(1,128)} %all-gather.19.cloned.1.call-done) | data formatting | bytes 4194304 | tf_op jit(solution)/shard_map/all_gather | solution.py:28
  109.5 5.6 %copy.238 = f32[128,64,64]{2,1,0:T(8,128)} copy(f32[128,64,64]{0,2,1:T(8,128)} %bitcast.158) | data formatting | bytes 4194304 | tf_op jit(solution)/shard_map/reshape | solution.py:32
  115.1 7.0 %fusion.16 = f32[128,64,32]{1,2,0:T(8,128)} fusion(f32[128,64,64]{2,1,0:T(8,128)} %copy.238, f32[128,64,32]{1,2,0:T(8,128)S(1)} %gather_fusion, pred[128]{0:T(512)(128)(4,1)S(1)} %compare_and_fusion.21), kind=kOutput, calls=%fused_computation.38 | convolution fusion | flops 100925440 | bytes 4194432 | tf_op jit(solution)/shard_map/krc,kcn->krn/dot_general | solution.py:43
  141.0 4.2 %collective-permute-done.1 = f32[1024,32]{0,1:T(8,128)S(1)} collective-permute-done((f32[1024,32]{0,1:T(8,128)S(1)}, f32[1024,32]{0,1:T(8,128)S(1)}, u32[]{:S(2)}, u32[]{:S(2)}) %collective-permute-start.1) | collective-permute-done | bytes 131104 | tf_op jit(solution)/shard_map/ppermute | solution.py:12
  155.8 8.0 %collective-permute-done.2 = f32[1024,32]{0,1:T(8,128)S(1)} collective-permute-done((f32[1024,32]{0,1:T(8,128)S(1)}, f32[1024,32]{0,1:T(8,128)S(1)}, u32[]{:S(2)}, u32[]{:S(2)}) %collective-permute-start.2) | collective-permute-done | bytes 131104 | tf_op jit(solution)/shard_map/ppermute | solution.py:12
  169.2 11.5 %all-gather.25.cloned.1.call-done = f32[1,1,1024,512]{3,2,1,0:T(8,128)} async-done(((f32[1,1,256,512]{3,2,1,0:T(8,128)}), f32[1,1,1024,512]{3,2,1,0:T(8,128)}) %all-gather.25.cloned.1.call-update) | async-done | bytes 2097168 | tf_op jit(solution)/shard_map/all_gather | solution.py:60
  183.6 7.6 %collective-permute-start.3 = (f32[1024,32]{0,1:T(8,128)S(1)}, f32[1024,32]{0,1:T(8,128)S(1)}, u32[]{:S(2)}, u32[]{:S(2)}) collective-permute-start(f32[1024,32]{0,1:T(8,128)S(1)} %fusion.31), channel_id=1, source_target_pairs={{0,32},{4,36},{8,40},{12,44},{16,48},{20,52},{24,56},{28,60},{32,0... | collective-permute-start | bytes 393224 | tf_op jit(solution)/shard_map/ppermute | solution.py:12
  191.3 11.9 %collective-permute-done.3 = f32[1024,32]{0,1:T(8,128)S(1)} collective-permute-done((f32[1024,32]{0,1:T(8,128)S(1)}, f32[1024,32]{0,1:T(8,128)S(1)}, u32[]{:S(2)}, u32[]{:S(2)}) %collective-permute-start.3) | collective-permute-done | bytes 131104 | tf_op jit(solution)/shard_map/ppermute | solution.py:12
  208.6 12.7 %all-gather.27.cloned.1.call-done = f32[1,1,1024,512]{3,2,1,0:T(8,128)} async-done(((f32[1,1,256,512]{3,2,1,0:T(8,128)}), f32[1,1,1024,512]{3,2,1,0:T(8,128)}) %all-gather.27.cloned.1.call-update) | async-done | bytes 2097168 | tf_op jit(solution)/shard_map/all_gather | solution.py:60
  224.2 12.8 %collective-permute-start.4 = (f32[1024,32]{0,1:T(8,128)S(1)}, f32[1024,32]{0,1:T(8,128)S(1)}, u32[]{:S(2)}, u32[]{:S(2)}) collective-permute-start(f32[1024,32]{0,1:T(8,128)S(1)} %fusion.37), channel_id=1, source_target_pairs={{0,64},{4,68},{8,72},{12,76},{16,80},{20,84},{24,88},{28,92},{32,9... | collective-permute-start | bytes 393224 | tf_op jit(solution)/shard_map/ppermute | solution.py:12
  237.0 3.7 %collective-permute-done.4 = f32[1024,32]{0,1:T(8,128)S(1)} collective-permute-done((f32[1024,32]{0,1:T(8,128)S(1)}, f32[1024,32]{0,1:T(8,128)S(1)}, u32[]{:S(2)}, u32[]{:S(2)}) %collective-permute-start.4) | collective-permute-done | bytes 131104 | tf_op jit(solution)/shard_map/ppermute | solution.py:12
  246.2 15.7 %all-gather.29.cloned.1.call-done = f32[1,1,1024,512]{3,2,1,0:T(8,128)} async-done(((f32[1,1,256,512]{3,2,1,0:T(8,128)}), f32[1,1,1024,512]{3,2,1,0:T(8,128)}) %all-gather.29.cloned.1.call-update) | async-done | bytes 2097168 | tf_op jit(solution)/shard_map/all_gather | solution.py:60
  267.3 4.6 %collective-permute-done.5 = f32[1024,32]{0,1:T(8,128)S(1)} collective-permute-done((f32[1024,32]{0,1:T(8,128)S(1)}, f32[1024,32]{0,1:T(8,128)S(1)}, u32[]{:S(2)}, u32[]{:S(2)}) %collective-permute-start.5) | collective-permute-done | bytes 131104 | tf_op jit(solution)/shard_map/ppermute | solution.py:12
  277.4 25.3 %all-gather.31.cloned.1.call-done = f32[1,1,1024,512]{3,2,1,0:T(8,128)} async-done(((f32[1,1,256,512]{3,2,1,0:T(8,128)}), f32[1,1,1024,512]{3,2,1,0:T(8,128)}) %all-gather.31.cloned.1.call-update) | async-done | bytes 2097168 | tf_op jit(solution)/shard_map/all_gather | solution.py:60
  305.6 4.0 %collective-permute-start.6 = (f32[1024,32]{0,1:T(8,128)S(1)}, f32[1024,32]{0,1:T(8,128)S(1)}, u32[]{:S(2)}, u32[]{:S(2)}) collective-permute-start(f32[1024,32]{0,1:T(8,128)S(1)} %fusion.49), channel_id=1, source_target_pairs={{0,256},{4,260},{8,264},{12,268},{16,272},{20,276},{24,280},{28,28... | collective-permute-start | bytes 393224 | tf_op jit(solution)/shard_map/ppermute | solution.py:12
  310.5 3.3 all-to-all-start.2
  319.6 23.8 %all-gather.33.cloned.1.call-done = f32[1,1,1024,512]{3,2,1,0:T(8,128)} async-done(((f32[1,1,256,512]{3,2,1,0:T(8,128)}), f32[1,1,1024,512]{3,2,1,0:T(8,128)}) %all-gather.33.cloned.1.call-update) | async-done | bytes 2097168 | tf_op jit(solution)/shard_map/all_gather | solution.py:60
  351.1 5.2 %all-to-all-done.3 = f32[4,256,32]{1,2,0:T(8,128)S(1)} async-done(((f32[4,256,32]{1,2,0:T(8,128)}), f32[4,256,32]{1,2,0:T(8,128)S(1)}, u32[]{:S(2)}, u32[]{:S(2)}) %all-to-all-start.3) | async-done | bytes 131104 | tf_op jit(solution)/shard_map/all_to_all | solution.py:16
  (173 shorter events, 93.6 us)
Async XLA Ops:
  7.2 96.7 %all-gather.19.cloned.1.call-start = ((), (), s32[]{:S(2)}) async-start(), calls=%async_computation.4 | async-start | bytes 2621440 | tf_op jit(solution)/shard_map/all_gather | solution.py:28
  9.6 125.2 %all-gather.21.cloned.1.call-start = ((), (), s32[]{:S(2)}) async-start(), calls=%async_computation.5 | async-start | bytes 2621440 | tf_op jit(solution)/shard_map/all_gather | solution.py:60
  13.5 3.3 copy-start.2
  13.6 137.0 %all-gather.23.cloned.1.call-start = ((), (), s32[]{:S(2)}) async-start(), calls=%async_computation.6 | async-start | bytes 2621440 | tf_op jit(solution)/shard_map/all_gather | solution.py:60
  14.3 166.4 %all-gather.25.cloned.1.call-start = ((), (), s32[]{:S(2)}) async-start(), calls=%async_computation.7 | async-start | bytes 2621440 | tf_op jit(solution)/shard_map/all_gather | solution.py:60
  14.9 206.4 %all-gather.27.cloned.1.call-start = ((), (), s32[]{:S(2)}) async-start(), calls=%async_computation.8 | async-start | bytes 2621440 | tf_op jit(solution)/shard_map/all_gather | solution.py:60
  15.5 246.4 %all-gather.29.cloned.1.call-start = ((), (), s32[]{:S(2)}) async-start(), calls=%async_computation.9 | async-start | bytes 2621440 | tf_op jit(solution)/shard_map/all_gather | solution.py:60
  16.0 286.6 %all-gather.31.cloned.1.call-start = ((), (), s32[]{:S(2)}) async-start(), calls=%async_computation.10 | async-start | bytes 2621440 | tf_op jit(solution)/shard_map/all_gather | solution.py:60
  16.8 23.9 %copy-start.4 = (s32[1,32]{1,0:T(1,128)S(1)}, s32[1,32]{1,0:T(1,128)}, u32[]{:S(2)}) copy-start(s32[1,32]{1,0:T(1,128)} %param.15) | copy-start | bytes 388
  16.8 24.0 %copy-start.5 = (s32[1,32]{1,0:T(1,128)S(1)}, s32[1,32]{1,0:T(1,128)}, u32[]{:S(2)}) copy-start(s32[1,32]{1,0:T(1,128)} %param.14) | copy-start | bytes 388
  16.8 33.2 %copy-start.3 = (s32[1,7,2,1024]{3,2,1,0:T(2,128)S(1)}, s32[1,7,2,1024]{3,2,1,0:T(2,128)}, u32[]{:S(2)}) copy-start(s32[1,7,2,1024]{3,2,1,0:T(2,128)} %param.16) | copy-start | bytes 172036
  18.4 58.9 %all-to-all-start = ((f32[1,128,1280]{2,0,1:T(1,128)}), f32[1,128,1280]{2,0,1:T(1,128)S(1)}, u32[]{:S(2)}, u32[]{:S(2)}) async-start(f32[1,128,1280]{2,0,1:T(1,128)} %copy.232), calls=%async_computation | async-start | bytes 1310720 | tf_op jit(solution)/shard_map/all_to_all | solution.py:34
  38.0 305.4 %all-gather.33.cloned.1.call-start = ((), (), s32[]{:S(2)}) async-start(), calls=%async_computation.11 | async-start | bytes 2621440 | tf_op jit(solution)/shard_map/all_gather | solution.py:60
  78.2 22.6 %all-to-all-start.1 = ((f32[4,32,1280]{2,1,0:T(8,128)}), f32[4,32,1280]{2,1,0:T(8,128)S(1)}, u32[]{:S(2)}, u32[]{:S(2)}) async-start(f32[4,32,1280]{2,1,0:T(8,128)} %bitcast.67), calls=%async_computation.1 | async-start | bytes 1310720 | tf_op jit(solution)/shard_map/all_to_all | solution.py:35
  122.1 3.6 %copy-start = (f32[32,4,256]{0,2,1:T(8,128)S(1)}, f32[32,4,256]{0,2,1:T(8,128)}, u32[]{:S(2)}) copy-start(f32[32,4,256]{0,2,1:T(8,128)} %copy.233) | copy-start | bytes 393220
  125.8 3.8 %collective-permute-start = (f32[1024,32]{1,0:T(8,128)S(1)}, f32[1024,32]{1,0:T(8,128)S(1)}, u32[]{:S(2)}, u32[]{:S(2)}) collective-permute-start(f32[1024,32]{1,0:T(8,128)S(1)} %bitcast_subtract_fusion), channel_id=1, source_target_pairs={{0,4},{4,0},{8,12},{12,8},{16,20},{20,16},{24,28},{28,24},{32,36},... | collective-permute-start | bytes 393224 | tf_op jit(solution)/shard_map/ppermute | solution.py:12
  137.8 7.4 %collective-permute-start.1 = (f32[1024,32]{0,1:T(8,128)S(1)}, f32[1024,32]{0,1:T(8,128)S(1)}, u32[]{:S(2)}, u32[]{:S(2)}) collective-permute-start(f32[1024,32]{0,1:T(8,128)S(1)} %select_subtract_fusion), channel_id=1, source_target_pairs={{0,8},{4,12},{8,0},{12,4},{16,24},{20,28},{24,16},{28,20},{32,40},... | collective-permute-start | bytes 393224 | tf_op jit(solution)/shard_map/ppermute | solution.py:12
  153.5 10.3 %collective-permute-start.2 = (f32[1024,32]{0,1:T(8,128)S(1)}, f32[1024,32]{0,1:T(8,128)S(1)}, u32[]{:S(2)}, u32[]{:S(2)}) collective-permute-start(f32[1024,32]{0,1:T(8,128)S(1)} %fusion.25), channel_id=1, source_target_pairs={{0,16},{4,20},{8,24},{12,28},{16,0},{20,4},{24,8},{28,12},{32,48},... | collective-permute-start | bytes 393224 | tf_op jit(solution)/shard_map/ppermute | solution.py:12
  183.6 19.6 %collective-permute-start.3 = (f32[1024,32]{0,1:T(8,128)S(1)}, f32[1024,32]{0,1:T(8,128)S(1)}, u32[]{:S(2)}, u32[]{:S(2)}) collective-permute-start(f32[1024,32]{0,1:T(8,128)S(1)} %fusion.31), channel_id=1, source_target_pairs={{0,32},{4,36},{8,40},{12,44},{16,48},{20,52},{24,56},{28,60},{32,0... | collective-permute-start | bytes 393224 | tf_op jit(solution)/shard_map/ppermute | solution.py:12
  224.2 16.6 %collective-permute-start.4 = (f32[1024,32]{0,1:T(8,128)S(1)}, f32[1024,32]{0,1:T(8,128)S(1)}, u32[]{:S(2)}, u32[]{:S(2)}) collective-permute-start(f32[1024,32]{0,1:T(8,128)S(1)} %fusion.37), channel_id=1, source_target_pairs={{0,64},{4,68},{8,72},{12,76},{16,80},{20,84},{24,88},{28,92},{32,9... | collective-permute-start | bytes 393224 | tf_op jit(solution)/shard_map/ppermute | solution.py:12
  264.8 7.1 %collective-permute-start.5 = (f32[1024,32]{0,1:T(8,128)S(1)}, f32[1024,32]{0,1:T(8,128)S(1)}, u32[]{:S(2)}, u32[]{:S(2)}) collective-permute-start(f32[1024,32]{0,1:T(8,128)S(1)} %fusion.43), channel_id=1, source_target_pairs={{0,128},{4,132},{8,136},{12,140},{16,144},{20,148},{24,152},{28,15... | collective-permute-start | bytes 393224 | tf_op jit(solution)/shard_map/ppermute | solution.py:12
  305.6 8.6 %collective-permute-start.6 = (f32[1024,32]{0,1:T(8,128)S(1)}, f32[1024,32]{0,1:T(8,128)S(1)}, u32[]{:S(2)}, u32[]{:S(2)}) collective-permute-start(f32[1024,32]{0,1:T(8,128)S(1)} %fusion.49), channel_id=1, source_target_pairs={{0,256},{4,260},{8,264},{12,268},{16,272},{20,276},{24,280},{28,28... | collective-permute-start | bytes 393224 | tf_op jit(solution)/shard_map/ppermute | solution.py:12
  310.5 36.5 %all-to-all-start.2 = ((f32[4,256,32]{1,2,0:T(8,128)}), f32[4,256,32]{1,2,0:T(8,128)S(1)}, u32[]{:S(2)}, u32[]{:S(2)}) async-start(f32[4,256,32]{1,2,0:T(8,128)} %copy.240), calls=%async_computation.2 | async-start | bytes 262144 | tf_op jit(solution)/shard_map/all_to_all | solution.py:16
  347.0 9.3 %all-to-all-start.3 = ((f32[4,256,32]{1,2,0:T(8,128)}), f32[4,256,32]{1,2,0:T(8,128)S(1)}, u32[]{:S(2)}, u32[]{:S(2)}) async-start(f32[4,256,32]{1,2,0:T(8,128)} %bitcast.157), calls=%async_computation.3 | async-start | bytes 262144 | tf_op jit(solution)/shard_map/all_to_all | solution.py:16
  (1 other events, 3.3 us)
Sparse Core Ops, SparseCore 0:
  10.1 42.9 all-gather.18
  55.2 45.4 all-gather.20
  102.8 37.2 all-gather.22
  142.1 38.5 all-gather.24
  182.7 38.5 all-gather.26
  223.2 38.5 all-gather.28
  264.0 38.6 all-gather.30
  304.8 38.6 all-gather.32
where the time goes:
time: 365 us; the launch traced here: 364 us
  waiting for transfers between devices  177 us (48%)
  local copies, waits for them, and re-layouts  68 us (19%)
  starting transfers between devices  65.1 us (18%)
  matrix products  27.6 us (8%)
  between operations  16.1 us (4%)
  blocking collectives  9.04 us (2%)
    all_gather x7, waiting for transfers between devices, on_device(): lax.all_gather(merge_maps[0, level - 1], 'case', axis=0, tiled=True)  89 us
    ppermute x7, waiting for transfers between devices, from_partner(): return lax.ppermute(value, axis, pairs)  34.6 us
    ppermute x7, starting transfers between devices, from_partner(): return lax.ppermute(value, axis, pairs)  34.3 us
    all_to_all x1, waiting for transfers between devices, on_device(): lax.all_to_all(joined, 'sub', split_axis=1, concat_axis=0, tiled=True)  26.4 us
    gather x14, local copies, waits for them, and re-layouts, on_device(): jnp.take(stacked, kept_index, axis=0)  20.9 us
    dot_general x7, matrix products, on_device(): jnp.dot(matrix, shared, precision=lax.Precision.HIGH)  20.2 us
    all_to_all x1, starting transfers between devices, on_device(): lax.all_to_all(joined, 'sub', split_axis=1, concat_axis=0, tiled=True)  19.6 us
    all_to_all x1, waiting for transfers between devices, on_device(): lax.all_to_all(joined, 'case', split_axis=0, concat_axis=1, tiled=True)  18.3 us
  transfers between devices with their start and end apart: 19, of which 15 were waited for; matrix products, arithmetic and copies ran while one was open for 26% of the time, Pallas kernels for 0%

commit v1 on v0

--- a/solution.py
+++ b/solution.py
@@ -27,7 +27,8 @@
     block_size = BLK
     blocks = lax.all_gather(cond_blocks[0], "case", axis=0, tiled=True)
     rows_of_blocks = lax.all_gather(block_rows[0], "case", axis=0, tiled=True)
-    cols_of_blocks = lax.all_gather(block_cols[0], "case", axis=0, tiled=True)
+    copies = jnp.concatenate([block_cols[0]] * lax.axis_size("case"), axis=0)
+    cols_of_blocks = lax.all_to_all(copies, "case", 0, 0, tiled=True)
     block_count = blocks.shape[0]
     blocks = blocks.reshape(block_count, block_size, block_size)
     joined = jnp.concatenate([load_interior, load_boundary], axis=2)

time: 365 us -> 367 us (level)
  waiting for transfers between devices: 177 us -> 170 us
  starting transfers between devices: 65.1 us -> 71.3 us
    unnamed x0 -> x1, blocking collectives: none -> 9.36 us
    all_gather x1 -> x0, blocking collectives: 9.04 us -> none  [on_device(): cols_of_blocks = lax.all_gather(block_cols[0], 'case', axis=0, tiled=True)]
    all_to_all x1, waiting for transfers between devices: 18.3 us -> 10.1 us  [on_device(): lax.all_to_all(joined, 'case', split_axis=0, concat_axis=1, tiled=True)]
    all_to_all x0 -> x1, starting transfers between devices: none -> 4.29 us  [on_device(): cols_of_blocks = lax.all_to_all(copies, 'case', 0, 0, tiled=True)]
  transfers between devices with their start and end apart: 19 -> 20, of which waited for: 15 -> 16; matrix products, arithmetic and copies ran while one was open for 26% -> 26% of each run, Pallas kernels for 0% -> 0%
where the time goes in v1:
time: 367 us; the launch traced here: 365 us
  waiting for transfers between devices  170 us (46%)
  starting transfers between devices  71.3 us (19%)
  local copies, waits for them, and re-layouts  69.3 us (19%)
  matrix products  27.6 us (8%)
  between operations  16.1 us (4%)
  blocking collectives  9.36 us (3%)
    all_gather x7, waiting for transfers between devices, on_device(): lax.all_gather(merge_maps[0, level - 1], 'case', axis=0, tiled=True)  89.8 us
    ppermute x7, starting transfers between devices, from_partner(): return lax.ppermute(value, axis, pairs)  35.7 us
    ppermute x7, waiting for transfers between devices, from_partner(): return lax.ppermute(value, axis, pairs)  33.2 us
    all_to_all x1, waiting for transfers between devices, on_device(): lax.all_to_all(joined, 'sub', split_axis=1, concat_axis=0, tiled=True)  28.4 us
    gather x14, local copies, waits for them, and re-layouts, on_device(): jnp.take(stacked, kept_index, axis=0)  20.9 us
    dot_general x7, matrix products, on_device(): jnp.dot(matrix, shared, precision=lax.Precision.HIGH)  20.2 us
    all_to_all x1, starting transfers between devices, on_device(): lax.all_to_all(joined, 'sub', split_axis=1, concat_axis=0, tiled=True)  19.6 us
    all_to_all x1, waiting for transfers between devices, on_device(): lax.all_to_all(joined, 'case', split_axis=0, concat_axis=1, tiled=True)  10.1 us
  transfers between devices with their start and end apart: 20, of which 16 were waited for; matrix products, arithmetic and copies ran while one was open for 26% of the time, Pallas kernels for 0%

profile of v1, /device:TPU:8, one launch (start us, length us, event | category | flops | bytes accessed | tf_op | source)
XLA Modules:
  0.0 365.4 jit_solution(17812728118371029978)
XLA Ops:
  9.7 3.9 %fusion.111 = (f32[1,1,256,512]{3,2,1,0:T(8,128)}, f32[1,1,256,512]{3,2,1,0:T(8,128)}, f32[1,1,256,512]{3,2,1,0:T(8,128)}, f32[1,1,256,512]{3,2,1,0:T(8,128)}, f...) fusion(f32[1,7,256,512]{3,2,1,0:T(8,128)} %param.17), kind=kLoop, calls=%fused_computation.217 | loop fusion | bytes 7340032 | tf_op jit(solution)/shard_map/slice | solution.py:61
  17.4 4.3 %all-to-all-start.2 = ((s32[4,32,1]{1,2,0:T(1,128)}), s32[4,32,1]{1,2,0:T(1,128)S(1)}, u32[]{:S(2)}, u32[]{:S(2)}) async-start(s32[4,32,1]{1,2,0:T(1,128)} %concatenate.53), calls=%async_computation.2 | async-start | bytes 4096 | tf_op jit(solution)/shard_map/all_to_all | solution.py:31
  26.9 19.6 %all-to-all-start = ((f32[1,128,1280]{2,0,1:T(1,128)}), f32[1,128,1280]{2,0,1:T(1,128)S(1)}, u32[]{:S(2)}, u32[]{:S(2)}) async-start(f32[1,128,1280]{2,0,1:T(1,128)} %copy.232), calls=%async_computation | async-start | bytes 1310720 | tf_op jit(solution)/shard_map/all_to_all | solution.py:35
  46.5 9.4 %all-reduce = s32[128]{0:T(128)S(1)} all-reduce(s32[128]{0:T(128)S(1)} %bitcast_dynamic-update-slice_fusion), channel_id=2, replica_groups=mesh['sub'=128,'case'=4] {'case'}, use_global_device_ids=true, to_apply=%add | all-reduce | flops 128 | bytes 1024
  57.4 28.4 %all-to-all-done = f32[1,128,1280]{2,0,1:T(1,128)S(1)} async-done(((f32[1,128,1280]{2,0,1:T(1,128)}), f32[1,128,1280]{2,0,1:T(1,128)S(1)}, u32[]{:S(2)}, u32[]{:S(2)}) %all-to-all-start) | async-done | bytes 655392 | tf_op jit(solution)/shard_map/all_to_all | solution.py:35
  86.7 4.7 %all-to-all-start.1 = ((f32[4,32,1280]{2,1,0:T(8,128)}), f32[4,32,1280]{2,1,0:T(8,128)S(1)}, u32[]{:S(2)}, u32[]{:S(2)}) async-start(f32[4,32,1280]{2,1,0:T(8,128)} %bitcast.68), calls=%async_computation.1 | async-start | bytes 1310720 | tf_op jit(solution)/shard_map/all_to_all | solution.py:36
  91.4 10.1 %all-to-all-done.1 = f32[4,32,1280]{2,1,0:T(8,128)S(1)} async-done(((f32[4,32,1280]{2,1,0:T(8,128)}), f32[4,32,1280]{2,1,0:T(8,128)S(1)}, u32[]{:S(2)}, u32[]{:S(2)}) %all-to-all-start.1) | async-done | bytes 655392 | tf_op jit(solution)/shard_map/all_to_all | solution.py:36
  104.5 5.6 %copy.237 = f32[1,128,4096]{1,2,0:T(8,128)} copy(f32[1,128,4096]{2,0,1:T(1,128)} %all-gather.18.cloned.1.call-done) | data formatting | bytes 4194304 | tf_op jit(solution)/shard_map/all_gather | solution.py:28
  110.2 5.6 %copy.238 = f32[128,64,64]{2,1,0:T(8,128)} copy(f32[128,64,64]{0,2,1:T(8,128)} %bitcast.161) | data formatting | bytes 4194304 | tf_op jit(solution)/shard_map/reshape | solution.py:33
  115.8 7.0 %fusion.16 = f32[128,64,32]{1,2,0:T(8,128)} fusion(f32[128,64,64]{2,1,0:T(8,128)} %copy.238, f32[128,64,32]{1,2,0:T(8,128)S(1)} %gather_fusion, pred[128]{0:T(512)(128)(4,1)S(1)} %compare_and_fusion.21), kind=kOutput, calls=%fused_computation.38 | convolution fusion | flops 100925440 | bytes 4194432 | tf_op jit(solution)/shard_map/krc,kcn->krn/dot_general | solution.py:44
  141.3 4.5 %collective-permute-done.1 = f32[1024,32]{0,1:T(8,128)S(1)} collective-permute-done((f32[1024,32]{0,1:T(8,128)S(1)}, f32[1024,32]{0,1:T(8,128)S(1)}, u32[]{:S(2)}, u32[]{:S(2)}) %collective-permute-start.1) | collective-permute-done | bytes 131104 | tf_op jit(solution)/shard_map/ppermute | solution.py:12
  154.2 3.9 %collective-permute-start.2 = (f32[1024,32]{0,1:T(8,128)S(1)}, f32[1024,32]{0,1:T(8,128)S(1)}, u32[]{:S(2)}, u32[]{:S(2)}) collective-permute-start(f32[1024,32]{0,1:T(8,128)S(1)} %fusion.25), channel_id=1, source_target_pairs={{0,16},{4,20},{8,24},{12,28},{16,0},{20,4},{24,8},{28,12},{32,48},... | collective-permute-start | bytes 393224 | tf_op jit(solution)/shard_map/ppermute | solution.py:12
  158.2 6.4 %collective-permute-done.2 = f32[1024,32]{0,1:T(8,128)S(1)} collective-permute-done((f32[1024,32]{0,1:T(8,128)S(1)}, f32[1024,32]{0,1:T(8,128)S(1)}, u32[]{:S(2)}, u32[]{:S(2)}) %collective-permute-start.2) | collective-permute-done | bytes 131104 | tf_op jit(solution)/shard_map/ppermute | solution.py:12
  170.0 12.2 %all-gather.24.cloned.1.call-done = f32[1,1,1024,512]{3,2,1,0:T(8,128)} async-done(((f32[1,1,256,512]{3,2,1,0:T(8,128)}), f32[1,1,1024,512]{3,2,1,0:T(8,128)}) %all-gather.24.cloned.1.call-update) | async-done | bytes 2097168 | tf_op jit(solution)/shard_map/all_gather | solution.py:61
  185.1 7.6 %collective-permute-start.3 = (f32[1024,32]{0,1:T(8,128)S(1)}, f32[1024,32]{0,1:T(8,128)S(1)}, u32[]{:S(2)}, u32[]{:S(2)}) collective-permute-start(f32[1024,32]{0,1:T(8,128)S(1)} %fusion.31), channel_id=1, source_target_pairs={{0,32},{4,36},{8,40},{12,44},{16,48},{20,52},{24,56},{28,60},{32,0... | collective-permute-start | bytes 393224 | tf_op jit(solution)/shard_map/ppermute | solution.py:12
  192.8 11.9 %collective-permute-done.3 = f32[1024,32]{0,1:T(8,128)S(1)} collective-permute-done((f32[1024,32]{0,1:T(8,128)S(1)}, f32[1024,32]{0,1:T(8,128)S(1)}, u32[]{:S(2)}, u32[]{:S(2)}) %collective-permute-start.3) | collective-permute-done | bytes 131104 | tf_op jit(solution)/shard_map/ppermute | solution.py:12
  210.1 12.7 %all-gather.26.cloned.1.call-done = f32[1,1,1024,512]{3,2,1,0:T(8,128)} async-done(((f32[1,1,256,512]{3,2,1,0:T(8,128)}), f32[1,1,1024,512]{3,2,1,0:T(8,128)}) %all-gather.26.cloned.1.call-update) | async-done | bytes 2097168 | tf_op jit(solution)/shard_map/all_gather | solution.py:61
  225.7 12.8 %collective-permute-start.4 = (f32[1024,32]{0,1:T(8,128)S(1)}, f32[1024,32]{0,1:T(8,128)S(1)}, u32[]{:S(2)}, u32[]{:S(2)}) collective-permute-start(f32[1024,32]{0,1:T(8,128)S(1)} %fusion.37), channel_id=1, source_target_pairs={{0,64},{4,68},{8,72},{12,76},{16,80},{20,84},{24,88},{28,92},{32,9... | collective-permute-start | bytes 393224 | tf_op jit(solution)/shard_map/ppermute | solution.py:12
  247.7 15.7 %all-gather.28.cloned.1.call-done = f32[1,1,1024,512]{3,2,1,0:T(8,128)} async-done(((f32[1,1,256,512]{3,2,1,0:T(8,128)}), f32[1,1,1024,512]{3,2,1,0:T(8,128)}) %all-gather.28.cloned.1.call-update) | async-done | bytes 2097168 | tf_op jit(solution)/shard_map/all_gather | solution.py:61
  268.7 4.6 %collective-permute-done.5 = f32[1024,32]{0,1:T(8,128)S(1)} collective-permute-done((f32[1024,32]{0,1:T(8,128)S(1)}, f32[1024,32]{0,1:T(8,128)S(1)}, u32[]{:S(2)}, u32[]{:S(2)}) %collective-permute-start.5) | collective-permute-done | bytes 131104 | tf_op jit(solution)/shard_map/ppermute | solution.py:12
  278.8 25.3 %all-gather.30.cloned.1.call-done = f32[1,1,1024,512]{3,2,1,0:T(8,128)} async-done(((f32[1,1,256,512]{3,2,1,0:T(8,128)}), f32[1,1,1024,512]{3,2,1,0:T(8,128)}) %all-gather.30.cloned.1.call-update) | async-done | bytes 2097168 | tf_op jit(solution)/shard_map/all_gather | solution.py:61
  307.0 4.0 %collective-permute-start.6 = (f32[1024,32]{0,1:T(8,128)S(1)}, f32[1024,32]{0,1:T(8,128)S(1)}, u32[]{:S(2)}, u32[]{:S(2)}) collective-permute-start(f32[1024,32]{0,1:T(8,128)S(1)} %fusion.49), channel_id=1, source_target_pairs={{0,256},{4,260},{8,264},{12,268},{16,272},{20,276},{24,280},{28,28... | collective-permute-start | bytes 393224 | tf_op jit(solution)/shard_map/ppermute | solution.py:12
  321.1 23.8 %all-gather.32.cloned.1.call-done = f32[1,1,1024,512]{3,2,1,0:T(8,128)} async-done(((f32[1,1,256,512]{3,2,1,0:T(8,128)}), f32[1,1,1024,512]{3,2,1,0:T(8,128)}) %all-gather.32.cloned.1.call-update) | async-done | bytes 2097168 | tf_op jit(solution)/shard_map/all_gather | solution.py:61
  352.6 5.2 %all-to-all-done.4 = f32[4,256,32]{1,2,0:T(8,128)S(1)} async-done(((f32[4,256,32]{1,2,0:T(8,128)}), f32[4,256,32]{1,2,0:T(8,128)S(1)}, u32[]{:S(2)}, u32[]{:S(2)}) %all-to-all-start.4) | async-done | bytes 131104 | tf_op jit(solution)/shard_map/all_to_all | solution.py:16
  (178 shorter events, 100.1 us)
Async XLA Ops:
  7.2 97.4 %all-gather.18.cloned.1.call-start = ((), (), s32[]{:S(2)}) async-start(), calls=%async_computation.5 | async-start | bytes 2621440 | tf_op jit(solution)/shard_map/all_gather | solution.py:28
  9.6 125.9 %all-gather.20.cloned.1.call-start = ((), (), s32[]{:S(2)}) async-start(), calls=%async_computation.6 | async-start | bytes 2621440 | tf_op jit(solution)/shard_map/all_gather | solution.py:61
  13.6 9.1 %copy-start.3 = (s32[1,7,2,1024]{3,2,1,0:T(2,128)S(1)}, s32[1,7,2,1024]{3,2,1,0:T(2,128)}, u32[]{:S(2)}) copy-start(s32[1,7,2,1024]{3,2,1,0:T(2,128)} %param.16) | copy-start | bytes 172036
  13.6 9.6 %copy-start.1 = (f32[1,128,1024]{2,1,0:T(8,128)S(1)}, f32[1,128,1024]{2,1,0:T(8,128)}, u32[]{:S(2)}) copy-start(f32[1,128,1024]{2,1,0:T(8,128)} %param.11) | copy-start | bytes 1572868
  13.6 9.6 %copy-start.2 = (f32[1,128,256]{2,1,0:T(8,128)S(1)}, f32[1,128,256]{2,1,0:T(8,128)}, u32[]{:S(2)}) copy-start(f32[1,128,256]{2,1,0:T(8,128)} %param.12) | copy-start | bytes 393220
  13.6 137.7 %all-gather.22.cloned.1.call-start = ((), (), s32[]{:S(2)}) async-start(), calls=%async_computation.7 | async-start | bytes 2621440 | tf_op jit(solution)/shard_map/all_gather | solution.py:61
  14.3 167.8 %all-gather.24.cloned.1.call-start = ((), (), s32[]{:S(2)}) async-start(), calls=%async_computation.8 | async-start | bytes 2621440 | tf_op jit(solution)/shard_map/all_gather | solution.py:61
  14.9 207.8 %all-gather.26.cloned.1.call-start = ((), (), s32[]{:S(2)}) async-start(), calls=%async_computation.9 | async-start | bytes 2621440 | tf_op jit(solution)/shard_map/all_gather | solution.py:61
  15.0 10.2 %copy-start.5 = (s32[1,32]{1,0:T(1,128)S(1)}, s32[1,32]{1,0:T(1,128)}, u32[]{:S(2)}) copy-start(s32[1,32]{1,0:T(1,128)} %param.14) | copy-start | bytes 388
  15.5 247.8 %all-gather.28.cloned.1.call-start = ((), (), s32[]{:S(2)}) async-start(), calls=%async_computation.10 | async-start | bytes 2621440 | tf_op jit(solution)/shard_map/all_gather | solution.py:61
  16.1 288.1 %all-gather.30.cloned.1.call-start = ((), (), s32[]{:S(2)}) async-start(), calls=%async_computation.11 | async-start | bytes 2621440 | tf_op jit(solution)/shard_map/all_gather | solution.py:61
  17.4 9.5 %all-to-all-start.2 = ((s32[4,32,1]{1,2,0:T(1,128)}), s32[4,32,1]{1,2,0:T(1,128)S(1)}, u32[]{:S(2)}, u32[]{:S(2)}) async-start(s32[4,32,1]{1,2,0:T(1,128)} %concatenate.53), calls=%async_computation.2 | async-start | bytes 4096 | tf_op jit(solution)/shard_map/all_to_all | solution.py:31
  21.7 323.2 %all-gather.32.cloned.1.call-start = ((), (), s32[]{:S(2)}) async-start(), calls=%async_computation.12 | async-start | bytes 2621440 | tf_op jit(solution)/shard_map/all_gather | solution.py:61
  26.9 58.9 %all-to-all-start = ((f32[1,128,1280]{2,0,1:T(1,128)}), f32[1,128,1280]{2,0,1:T(1,128)S(1)}, u32[]{:S(2)}, u32[]{:S(2)}) async-start(f32[1,128,1280]{2,0,1:T(1,128)} %copy.232), calls=%async_computation | async-start | bytes 1310720 | tf_op jit(solution)/shard_map/all_to_all | solution.py:35
  86.7 14.8 %all-to-all-start.1 = ((f32[4,32,1280]{2,1,0:T(8,128)}), f32[4,32,1280]{2,1,0:T(8,128)S(1)}, u32[]{:S(2)}, u32[]{:S(2)}) async-start(f32[4,32,1280]{2,1,0:T(8,128)} %bitcast.68), calls=%async_computation.1 | async-start | bytes 1310720 | tf_op jit(solution)/shard_map/all_to_all | solution.py:36
  126.5 3.8 %collective-permute-start = (f32[1024,32]{1,0:T(8,128)S(1)}, f32[1024,32]{1,0:T(8,128)S(1)}, u32[]{:S(2)}, u32[]{:S(2)}) collective-permute-start(f32[1024,32]{1,0:T(8,128)S(1)} %bitcast_subtract_fusion), channel_id=1, source_target_pairs={{0,4},{4,0},{8,12},{12,8},{16,20},{20,16},{24,28},{28,24},{32,36},... | collective-permute-start | bytes 393224 | tf_op jit(solution)/shard_map/ppermute | solution.py:12
  138.4 7.5 %collective-permute-start.1 = (f32[1024,32]{0,1:T(8,128)S(1)}, f32[1024,32]{0,1:T(8,128)S(1)}, u32[]{:S(2)}, u32[]{:S(2)}) collective-permute-start(f32[1024,32]{0,1:T(8,128)S(1)} %select_subtract_fusion), channel_id=1, source_target_pairs={{0,8},{4,12},{8,0},{12,4},{16,24},{20,28},{24,16},{28,20},{32,40},... | collective-permute-start | bytes 393224 | tf_op jit(solution)/shard_map/ppermute | solution.py:12
  154.2 10.3 %collective-permute-start.2 = (f32[1024,32]{0,1:T(8,128)S(1)}, f32[1024,32]{0,1:T(8,128)S(1)}, u32[]{:S(2)}, u32[]{:S(2)}) collective-permute-start(f32[1024,32]{0,1:T(8,128)S(1)} %fusion.25), channel_id=1, source_target_pairs={{0,16},{4,20},{8,24},{12,28},{16,0},{20,4},{24,8},{28,12},{32,48},... | collective-permute-start | bytes 393224 | tf_op jit(solution)/shard_map/ppermute | solution.py:12
  185.1 19.6 %collective-permute-start.3 = (f32[1024,32]{0,1:T(8,128)S(1)}, f32[1024,32]{0,1:T(8,128)S(1)}, u32[]{:S(2)}, u32[]{:S(2)}) collective-permute-start(f32[1024,32]{0,1:T(8,128)S(1)} %fusion.31), channel_id=1, source_target_pairs={{0,32},{4,36},{8,40},{12,44},{16,48},{20,52},{24,56},{28,60},{32,0... | collective-permute-start | bytes 393224 | tf_op jit(solution)/shard_map/ppermute | solution.py:12
  225.7 16.6 %collective-permute-start.4 = (f32[1024,32]{0,1:T(8,128)S(1)}, f32[1024,32]{0,1:T(8,128)S(1)}, u32[]{:S(2)}, u32[]{:S(2)}) collective-permute-start(f32[1024,32]{0,1:T(8,128)S(1)} %fusion.37), channel_id=1, source_target_pairs={{0,64},{4,68},{8,72},{12,76},{16,80},{20,84},{24,88},{28,92},{32,9... | collective-permute-start | bytes 393224 | tf_op jit(solution)/shard_map/ppermute | solution.py:12
  266.2 7.1 %collective-permute-start.5 = (f32[1024,32]{0,1:T(8,128)S(1)}, f32[1024,32]{0,1:T(8,128)S(1)}, u32[]{:S(2)}, u32[]{:S(2)}) collective-permute-start(f32[1024,32]{0,1:T(8,128)S(1)} %fusion.43), channel_id=1, source_target_pairs={{0,128},{4,132},{8,136},{12,140},{16,144},{20,148},{24,152},{28,15... | collective-permute-start | bytes 393224 | tf_op jit(solution)/shard_map/ppermute | solution.py:12
  307.0 8.6 %collective-permute-start.6 = (f32[1024,32]{0,1:T(8,128)S(1)}, f32[1024,32]{0,1:T(8,128)S(1)}, u32[]{:S(2)}, u32[]{:S(2)}) collective-permute-start(f32[1024,32]{0,1:T(8,128)S(1)} %fusion.49), channel_id=1, source_target_pairs={{0,256},{4,260},{8,264},{12,268},{16,272},{20,276},{24,280},{28,28... | collective-permute-start | bytes 393224 | tf_op jit(solution)/shard_map/ppermute | solution.py:12
  312.0 36.5 %all-to-all-start.3 = ((f32[4,256,32]{1,2,0:T(8,128)}), f32[4,256,32]{1,2,0:T(8,128)S(1)}, u32[]{:S(2)}, u32[]{:S(2)}) async-start(f32[4,256,32]{1,2,0:T(8,128)} %copy.240), calls=%async_computation.3 | async-start | bytes 262144 | tf_op jit(solution)/shard_map/all_to_all | solution.py:16
  348.5 9.3 %all-to-all-start.4 = ((f32[4,256,32]{1,2,0:T(8,128)}), f32[4,256,32]{1,2,0:T(8,128)S(1)}, u32[]{:S(2)}, u32[]{:S(2)}) async-start(f32[4,256,32]{1,2,0:T(8,128)} %bitcast.160), calls=%async_computation.4 | async-start | bytes 262144 | tf_op jit(solution)/shard_map/all_to_all | solution.py:16
  (2 other events, 6.9 us)
Sparse Core Ops, SparseCore 0:
  10.1 42.8 all-gather.17
  55.1 38.6 all-gather.19
  95.9 45.6 all-gather.21
  143.5 38.5 all-gather.23
  184.1 38.5 all-gather.25
  224.7 38.5 all-gather.27
  265.4 38.6 all-gather.29
  306.2 38.6 all-gather.31
